TPU v7x, 32 devices: a whole 2x2x4 slice. The times are simulated.
32 devices in a mesh: slab: 8 (over y, x, core), view: 4 (over z).
Axes of the slice: x: 2, y: 2, z: 4, core: 2. Of those that a mesh axis runs over, the one named last changes fastest.
Arguments:
- estimate: float32 [4, 1024, 1024], P(None, 'slab'), may hold values from 0.5 to 2
- views: float32 [4, 4, 1024, 1024], P('view', None, 'slab'), may hold values from 0.25 to 4
- psf: float32 [4, 1024, 1024], P('view', 'slab'), as said below
- pattern_mult: int32 [4, 8], P('view'), may hold values from 0 to 63
- pattern_shift: int32 [4, 8], P('view'), may hold values from 0 to 127
- interp: float32 [4, 8, 128], P('view'), may hold values from 0.05 to 0.45
Outputs:
- updated: float32 [4, 1024, 1024], P(None, 'slab')
Inputs may be any that keep to these rules, and one draw needn't show every extreme that they name: `psf`: every entry is positive.
All inputs are finite; a program needn't handle non-finite values.
Results may differ from a plain program's by a relative error of at most 0.0001.
Values sent between devices are 32-bit elements; how exact they have to be, the bound alone decides.
No kernel may reach another device: no remote copies, remote signals or barrier semaphores. Data moves between devices by JAX's collectives and lax.ppermute only.
A program may use at most 128 MiB of HBM per device.

v0:
```python
import math
import jax
import jax.numpy as jnp
from jax import lax
from jax.sharding import PartitionSpec as P

highest = lax.Precision.HIGHEST


def block_matrix(multiplier, shifting, weights):
    positions = jnp.arange(128, dtype=jnp.int32)
    first_col = ((2 * multiplier[:, None] + 1) * positions[None, :] + shifting[:, None]) % 128
    second_col = (first_col + 1) % 128
    columns = positions[None, None, :]
    lower = (columns == first_col[:, :, None]).astype(jnp.float32)
    upper = (columns == second_col[:, :, None]).astype(jnp.float32)
    return (1.0 - weights)[:, :, None] * lower + weights[:, :, None] * upper


def angle_tables(rows, cols, length):
    row_index = lax.iota(jnp.int32, rows)[:, None]
    col_index = lax.iota(jnp.int32, cols)[None, :]
    angles = (row_index * col_index % length).astype(jnp.float32) * (2.0 * math.pi / length)
    return (jnp.cos(angles), jnp.sin(angles))


def unit_root(numerator, length):
    angle = 2.0 * math.pi * numerator / length
    return (round(math.cos(angle), 15), round(math.sin(angle), 15))


def small_stage(real_part, imag_part, axis, direction):
    count = real_part.shape[axis]

    def part(array, index):
        return lax.index_in_dim(array, index, axis, keepdims=False)

    real_in = [part(real_part, index) for index in range(count)]
    imag_in = None if imag_part is None else [part(imag_part, index) for index in range(count)]
    real_out, imag_out = ([], [])
    for out_index in range(count):
        real_sum, imag_sum = (None, None)
        for in_index in range(count):
            cosine, sine = unit_root(in_index * out_index, count)
            sine = direction * sine
            terms_real = []
            terms_imag = []
            if cosine != 0.0:
                terms_real.append(cosine * real_in[in_index])
                if imag_in is not None:
                    terms_imag.append(cosine * imag_in[in_index])
            if sine != 0.0:
                terms_imag.append(sine * real_in[in_index])
                if imag_in is not None:
                    terms_real.append(-sine * imag_in[in_index])
            for term in terms_real:
                real_sum = term if real_sum is None else real_sum + term
            for term in terms_imag:
                imag_sum = term if imag_sum is None else imag_sum + term
        if imag_sum is None:
            imag_sum = jnp.zeros_like(real_sum)
        real_out.append(real_sum)
        imag_out.append(imag_sum)
    return (jnp.stack(real_out, axis), jnp.stack(imag_out, axis))


def complex_times(real_part, imag_part, cosine, sine_table):
    return (
        real_part * cosine - imag_part * sine_table,
        real_part * sine_table + imag_part * cosine,
    )


def block_dft_matrix(length, direction):
    cosine, sine = angle_tables(length, length, length)
    sine = direction * sine
    top = jnp.concatenate([cosine, sine], 1)
    bottom = jnp.concatenate([-sine, cosine], 1)
    return jnp.concatenate([top, bottom], 0)


def large_stage(real_part, imag_part, axis, direction):
    length = real_part.shape[axis]
    if imag_part is None:
        imag_part = jnp.zeros_like(real_part)
    joined = jnp.concatenate([real_part, imag_part], axis)
    matrix = block_dft_matrix(length, direction)
    if axis == joined.ndim - 1:
        out = jnp.einsum("...j,jn->...n", joined, matrix, precision=highest)
    else:
        out = jnp.einsum("rkjz,jn->rknz", joined, matrix, precision=highest)
    return (
        lax.slice_in_dim(out, 0, length, axis=axis),
        lax.slice_in_dim(out, length, 2 * length, axis=axis),
    )


def factored(real_part, imag_part, axis, direction, forward, want_imag=True):
    length = real_part.shape[axis]
    second = 128
    first = length // second
    outer = real_part.shape
    shape = outer[:axis] + (first, second) + outer[axis + 1 :]
    real_part = real_part.reshape(shape)
    if imag_part is not None:
        imag_part = imag_part.reshape(shape)
    twist_cos, twist_sin = angle_tables(first, second, length)
    if axis == 1:
        twist_cos = twist_cos[:, :, None]
        twist_sin = twist_sin[:, :, None]
    twist_sin = direction * twist_sin
    if forward:
        real_part, imag_part = small_stage(real_part, imag_part, axis, direction)
        real_part, imag_part = complex_times(real_part, imag_part, twist_cos, twist_sin)
        real_part, imag_part = large_stage(real_part, imag_part, axis + 1, direction)
    else:
        real_part, imag_part = large_stage(real_part, imag_part, axis + 1, direction)
        real_part, imag_part = complex_times(real_part, imag_part, twist_cos, twist_sin)
        real_part, imag_part = small_stage(real_part, imag_part, axis, direction)
    return (real_part.reshape(outer), imag_part.reshape(outer))


def to_columns(real_part, imag_part):
    depth_real, depth_imag = factored(real_part, imag_part, 2, -1.0, True)
    rows = depth_real.shape[0]
    stacked = jnp.concatenate([depth_real, depth_imag], 0)
    moved = lax.all_to_all(stacked, "slab", split_axis=2, concat_axis=1, tiled=True)
    return factored(moved[:rows], moved[rows:], 1, -1.0, True)


def to_planes(real_part, imag_part):
    width_real, width_imag = factored(real_part, imag_part, 1, 1.0, False)
    rows = width_real.shape[0]
    stacked = jnp.concatenate([width_real, width_imag], 0)
    moved = lax.all_to_all(stacked, "slab", split_axis=1, concat_axis=2, tiled=True)
    return factored(moved[:rows], moved[rows:], 2, 1.0, False)


def pack_pairs(volume):
    return (volume[0::2], volume[1::2])


def unpack_pairs(real_part, imag_part):
    pairs, width, depth = real_part.shape
    return jnp.stack([real_part, imag_part], 1).reshape(2 * pairs, width, depth)


def general_shards(estimate, views, psf, pattern_mult, pattern_shift, interp):
    row_count, slab_width, depth = estimate.shape
    blocks = block_matrix(pattern_mult[0], pattern_shift[0], interp[0])
    block_count = depth // 128
    shaped = estimate.reshape(row_count, slab_width, block_count, 128)
    sampled = jnp.einsum("bij,yxbj->yxbi", blocks, shaped, precision=highest).reshape(
        row_count, slab_width, depth
    )
    packed_real, packed_imag = pack_pairs(sampled)
    packed_real = jnp.concatenate([packed_real, psf], 0)
    packed_imag = jnp.concatenate([packed_imag, jnp.zeros_like(psf)], 0)
    spectra_real, spectra_imag = to_columns(packed_real, packed_imag)
    scaling = 1.0 / (spectra_real.shape[1] * depth)
    transfer_real = spectra_real[-1:] * scaling
    transfer_imag = spectra_imag[-1:] * scaling
    spectra_real = spectra_real[:-1]
    spectra_imag = spectra_imag[:-1]
    filtered_real = spectra_real * transfer_real - spectra_imag * transfer_imag
    filtered_imag = spectra_real * transfer_imag + spectra_imag * transfer_real
    blurred = unpack_pairs(*to_planes(filtered_real, filtered_imag))
    quotient = views[0] / blurred
    packed_real, packed_imag = pack_pairs(quotient)
    spectra_real, spectra_imag = to_columns(packed_real, packed_imag)
    filtered_real = spectra_real * transfer_real + spectra_imag * transfer_imag
    filtered_imag = spectra_imag * transfer_real - spectra_real * transfer_imag
    smeared = unpack_pairs(*to_planes(filtered_real, filtered_imag))
    correction = jnp.einsum(
        "bij,yxbi->yxbj",
        blocks,
        smeared.reshape(row_count, slab_width, block_count, 128),
        precision=highest,
    ).reshape(row_count, slab_width, depth)
    log_terms = jnp.log(correction)
    view_count = lax.axis_size("view")
    summed = lax.psum(log_terms, "view")
    return estimate * jnp.exp(summed / view_count)


def swap_halves(joined):
    half = joined.shape[-1] // 2
    return jnp.concatenate([-joined[..., half:], joined[..., :half]], -1)


def butterflies(parts, direction, turn):
    count = len(parts)
    if count == 1:
        return parts
    even = butterflies(parts[0::2], direction, turn)
    odd = butterflies(parts[1::2], direction, turn)
    out = [None] * count
    for index in range(count // 2):
        cosine, sine = unit_root(index, count)
        sine = direction * sine
        value = odd[index]
        if sine == 0.0:
            rotated = value if cosine > 0 else -value
        elif cosine == 0.0:
            rotated = turn(value) if sine > 0 else -turn(value)
        else:
            rotated = cosine * value + sine * turn(value)
        out[index] = even[index] + rotated
        out[index + count // 2] = even[index] - rotated
    return out


def lead_stage(joined, direction):
    count = joined.shape[0]
    parts = [joined[index] for index in range(count)]
    return jnp.stack(butterflies(parts, direction, swap_halves), 0)


def joined_twist(joined, length, direction, lanes):
    first, second = (joined.shape[0], joined.shape[-1] // 2 if lanes else joined.shape[2])
    cosine, sine = angle_tables(first, second, length)
    sine = direction * sine
    if lanes:
        cosine = jnp.concatenate([cosine, cosine], 1)[:, None, None, :]
        sine = jnp.concatenate([sine, sine], 1)[:, None, None, :]
    else:
        cosine = cosine[:, None, :, None]
        sine = sine[:, None, :, None]
    return joined * cosine + swap_halves(joined) * sine


def lane_stage(joined, direction):
    length = joined.shape[-1] // 2
    matrix = block_dft_matrix(length, direction)
    return jnp.einsum("...j,jn->...n", joined, matrix, precision=lax.Precision.HIGH)


def row_stage(joined, direction):
    length = joined.shape[2]
    cosine, sine = angle_tables(length, length, length)
    matrix = jnp.concatenate([cosine, direction * sine], 0)
    both = jnp.concatenate([joined, swap_halves(joined)], 2)
    return jnp.einsum("krjl,jm->krml", both, matrix, precision=lax.Precision.HIGH)


def depth_forward(joined, depth):
    joined = lead_stage(joined, -1.0)
    joined = joined_twist(joined, depth, -1.0, True)
    return lane_stage(joined, -1.0)


def depth_inverse(joined, depth):
    joined = lane_stage(joined, 1.0)
    joined = joined_twist(joined, depth, 1.0, True)
    return lead_stage(joined, 1.0)


def width_forward(joined, width):
    joined = lead_stage(joined, -1.0)
    joined = joined_twist(joined, width, -1.0, False)
    return row_stage(joined, -1.0)


def width_inverse(joined, width):
    joined = row_stage(joined, 1.0)
    joined = joined_twist(joined, width, 1.0, False)
    return lead_stage(joined, 1.0)


def joined_times(joined, transfer_real, transfer_imag):
    return joined * transfer_real + swap_halves(joined) * transfer_imag


def to_blocks(volume, block_count):
    rows, width, depth = volume.shape
    lanes = depth // block_count
    parity = [volume[0::2], volume[1::2]]
    return jnp.stack(
        [
            jnp.concatenate(
                [part[:, :, block * lanes : (block + 1) * lanes] for part in parity], -1
            )
            for block in range(block_count)
        ],
        0,
    )


def from_blocks(blocked):
    block_count, pairs, width, lanes = blocked.shape
    half = lanes // 2
    parity = [
        jnp.concatenate(
            [blocked[block, :, :, side * half : (side + 1) * half] for block in range(block_count)],
            -1,
        )
        for side in range(2)
    ]
    return jnp.stack(parity, 1).reshape(2 * pairs, width, block_count * half)


def shards(estimate, views, psf, pattern_mult, pattern_shift, interp):
    row_count, slab_width, depth = estimate.shape
    slab_count = lax.axis_size("slab")
    block_count = depth // 128
    width = slab_width * slab_count
    if not (
        block_count == slab_count
        and slab_width == 128
        and (width // 128 == slab_count)
        and (row_count % 2 == 0)
    ):
        return general_shards(estimate, views, psf, pattern_mult, pattern_shift, interp)
    blocks = block_matrix(pattern_mult[0], pattern_shift[0], interp[0])
    empty = jnp.zeros_like(blocks)
    doubled = jnp.concatenate(
        [jnp.concatenate([blocks, empty], 2), jnp.concatenate([empty, blocks], 2)], 1
    )
    sampled = jnp.einsum(
        "apxl,aml->apxm", to_blocks(estimate, block_count), doubled, precision=lax.Precision.HIGH
    )
    pairs = row_count // 2
    spread = psf.reshape(slab_width, block_count, 128).transpose(1, 0, 2)[:, None]
    spread = jnp.concatenate([spread, jnp.zeros_like(spread)], -1)

    def to_columns_blocked(planes):
        spectra = depth_forward(planes, depth)
        spectra = lax.all_to_all(spectra, "slab", split_axis=0, concat_axis=0, tiled=True)
        return width_forward(spectra, width)

    transfer = to_columns_blocked(spread) * (1.0 / (width * depth))
    spectra = to_columns_blocked(sampled)
    half = transfer.shape[-1] // 2
    transfer_real = jnp.concatenate([transfer[..., :half], transfer[..., :half]], -1)
    transfer_imag = jnp.concatenate([transfer[..., half:], transfer[..., half:]], -1)

    def convolve(spectra, transfer_imag):
        filtered = joined_times(spectra, transfer_real, transfer_imag)
        planes = width_inverse(filtered, width)
        planes = lax.all_to_all(planes, "slab", split_axis=0, concat_axis=0, tiled=True)
        return depth_inverse(planes, depth)

    blurred = convolve(spectra, transfer_imag)
    quotient = to_blocks(views[0], block_count) / blurred
    spectra = depth_forward(quotient, depth)
    spectra = lax.all_to_all(spectra, "slab", split_axis=0, concat_axis=0, tiled=True)
    spectra = width_forward(spectra, width)
    smeared = convolve(spectra, -transfer_imag)
    correction = jnp.einsum("apxm,aml->apxl", smeared, doubled, precision=lax.Precision.HIGH)
    log_terms = from_blocks(jnp.log(correction))
    view_count = lax.axis_size("view")
    summed = lax.psum(log_terms, "view")
    return estimate * jnp.exp(summed / view_count)


def solution(mesh):
    placed = (
        P(None, "slab", None),
        P("view", None, "slab", None),
        P("view", "slab", None),
        P("view", None),
        P("view", None),
        P("view", None, None),
    )
    return jax.shard_map(
        shards, mesh=mesh, in_specs=placed, out_specs=P(None, "slab", None), check_vma=False
    )
```

profile of v0, /device:TPU:0, one launch (start us, length us, event | category | flops | bytes accessed | tf_op | source)
XLA Modules:
  0.0 285.5 jit_solution(3338076680275577387)
XLA Ops:
  7.2 1.2 copy.41
  9.5 1.6 convolution_bitcast_fusion
  11.1 5.2 %all-to-all-start.1 = ((f32[8,1,128,256]{3,2,1,0:T(8,128)}), f32[8,1,128,256]{3,2,1,0:T(8,128)S(1)}, u32[]{:S(2)}, u32[]{:S(2)}) async-start(f32[8,1,128,256]{3,2,1,0:T(8,128)} %convolution_bitcast_fusion), calls=%async_computation.1 | async-start | bytes 2097152 | tf_op jit(solution)/shard_map/all_to_all | solution.py:328
  18.8 1.1 fusion.52
  21.4 2.4 fusion.26
  23.8 7.9 %all-to-all-done.1 = f32[8,1,128,256]{3,2,1,0:T(8,128)S(1)} async-done(((f32[8,1,128,256]{3,2,1,0:T(8,128)}), f32[8,1,128,256]{3,2,1,0:T(8,128)S(1)}, u32[]{:S(2)}, u32[]{:S(2)}) %all-to-all-start.1) | async-done | bytes 1048608 | tf_op jit(solution)/shard_map/all_to_all | solution.py:328
  31.7 3.8 %all-to-all-start = ((f32[8,2,128,256]{3,2,1,0:T(8,128)}), f32[8,2,128,256]{3,2,1,0:T(8,128)S(1)}, u32[]{:S(2)}, u32[]{:S(2)}) async-start(f32[8,2,128,256]{3,2,1,0:T(8,128)} %fusion.26), calls=%async_computation | async-start | bytes 4194304 | tf_op jit(solution)/shard_map/all_to_all | solution.py:328
  37.6 1.0 slice_bitcast_fusion.67
  38.6 1.0 maximum_bitcast_fusion.7
  39.7 22.2 %all-to-all-done = f32[8,2,128,256]{3,2,1,0:T(8,128)S(1)} async-done(((f32[8,2,128,256]{3,2,1,0:T(8,128)}), f32[8,2,128,256]{3,2,1,0:T(8,128)S(1)}, u32[]{:S(2)}, u32[]{:S(2)}) %all-to-all-start) | async-done | bytes 2097184 | tf_op jit(solution)/shard_map/all_to_all | solution.py:328
  63.8 1.6 fusion.66
  65.7 1.0 copy-done.3
  67.3 1.5 fusion.63
  69.4 0.9 subtract_bitcast_fusion.15
  76.1 3.8 %all-to-all-start.2 = ((f32[8,2,128,256]{3,2,1,0:T(8,128)}), f32[8,2,128,256]{3,2,1,0:T(8,128)S(1)}, u32[]{:S(2)}, u32[]{:S(2)}) async-start(f32[8,2,128,256]{3,2,1,0:T(8,128)} %subtract_dynamic-update-slice_fusion.20), calls=%async_computation.2 | async-start | bytes 4194304 | tf_op jit(solution)/shard_map/all_to_all | solution.py:340
  80.2 1.7 fusion.269
  88.0 18.4 %all-to-all-done.2 = f32[8,2,128,256]{3,2,1,0:T(8,128)S(1)} async-done(((f32[8,2,128,256]{3,2,1,0:T(8,128)}), f32[8,2,128,256]{3,2,1,0:T(8,128)S(1)}, u32[]{:S(2)}, u32[]{:S(2)}) %all-to-all-start.2) | async-done | bytes 2097184 | tf_op jit(solution)/shard_map/all_to_all | solution.py:340
  106.3 1.0 fusion.128
  109.0 2.0 div.9
  112.4 2.4 fusion.40
  114.8 3.6 %all-to-all-start.3 = ((f32[8,2,128,256]{3,2,1,0:T(8,128)}), f32[8,2,128,256]{3,2,1,0:T(8,128)S(1)}, u32[]{:S(2)}, u32[]{:S(2)}) async-start(f32[8,2,128,256]{3,2,1,0:T(8,128)} %fusion.40), calls=%async_computation.3 | async-start | bytes 4194304 | tf_op jit(solution)/shard_map/all_to_all | solution.py:346
  118.7 2.2 maximum_negate_fusion
  121.0 24.0 %all-to-all-done.3 = f32[8,2,128,256]{3,2,1,0:T(8,128)S(1)} async-done(((f32[8,2,128,256]{3,2,1,0:T(8,128)}), f32[8,2,128,256]{3,2,1,0:T(8,128)S(1)}, u32[]{:S(2)}, u32[]{:S(2)}) %all-to-all-start.3) | async-done | bytes 2097184 | tf_op jit(solution)/shard_map/all_to_all | solution.py:346
  147.0 1.6 fusion.60
  148.8 1.0 copy-done.2
  150.4 1.5 fusion.57
  153.7 29.0 %all_to_all.25 = f32[8,2,128,256]{3,2,1,0:T(8,128)S(1)} all-to-all(f32[8,2,128,256]{3,2,1,0:T(8,128)S(1)} %subtract_dynamic-update-slice_fusion.4), channel_id=1, replica_groups=mesh['slab'=8,'view'=4] {'slab'}, dimensions={0} | all-to-all | bytes 4194304 | tf_op jit(solution)/shard_map/all_to_all | solution.py:340
  182.8 1.0 fusion.126
  186.3 1.1 fusion.54
  187.9 1.5 copy.69
  189.3 86.0 %all-reduce.5.cloned.1.call-done = f32[4,128,1024]{2,1,0:T(8,128)} async-done(((f32[4,128,1024]{2,1,0:T(8,128)}), f32[4,128,1024]{2,1,0:T(8,128)}) %all-reduce.5.cloned.1.call-update) | async-done | bytes 2097168 | tf_op jit(solution)/shard_map/psum | solution.py:352
  275.4 3.3 %exponential_multiply_fusion = f32[4,128,1024]{2,1,0:T(8,128)} fusion(f32[4,128,1024]{2,1,0:T(8,128)S(1)} %copy-done.1, f32[4,128,1024]{2,1,0:T(8,128)} %all-reduce.5.cloned.1.call-done), kind=kLoop, calls=%fused_computation.69 | loop fusion | flops 1048576 | bytes 6291456 | tf_op jit(solution)/shard_map/mul | solution.py:353
  (245 shorter events, 33.3 us)
Async XLA Ops:
  9.5 7.0 %copy-start = (f32[4,128,1024]{2,1,0:T(8,128)S(1)}, f32[4,128,1024]{2,1,0:T(8,128)}, u32[]{:S(2)}) copy-start(f32[4,128,1024]{2,1,0:T(8,128)} %param.6) | copy-start | bytes 6291460
  11.1 20.6 %all-to-all-start.1 = ((f32[8,1,128,256]{3,2,1,0:T(8,128)}), f32[8,1,128,256]{3,2,1,0:T(8,128)S(1)}, u32[]{:S(2)}, u32[]{:S(2)}) async-start(f32[8,1,128,256]{3,2,1,0:T(8,128)} %convolution_bitcast_fusion), calls=%async_computation.1 | async-start | bytes 2097152 | tf_op jit(solution)/shard_map/all_to_all | solution.py:328
  16.5 0.7 copy-start.8
  16.6 0.7 copy-start.6
  17.3 0.7 copy-start.7
  18.8 1.1 copy-start.4
  31.7 30.2 %all-to-all-start = ((f32[8,2,128,256]{3,2,1,0:T(8,128)}), f32[8,2,128,256]{3,2,1,0:T(8,128)S(1)}, u32[]{:S(2)}, u32[]{:S(2)}) async-start(f32[8,2,128,256]{3,2,1,0:T(8,128)} %fusion.26), calls=%async_computation | async-start | bytes 4194304 | tf_op jit(solution)/shard_map/all_to_all | solution.py:328
  65.4 1.2 copy-start.3
  76.1 30.2 %all-to-all-start.2 = ((f32[8,2,128,256]{3,2,1,0:T(8,128)}), f32[8,2,128,256]{3,2,1,0:T(8,128)S(1)}, u32[]{:S(2)}, u32[]{:S(2)}) async-start(f32[8,2,128,256]{3,2,1,0:T(8,128)} %subtract_dynamic-update-slice_fusion.20), calls=%async_computation.2 | async-start | bytes 4194304 | tf_op jit(solution)/shard_map/all_to_all | solution.py:340
  114.8 30.2 %all-to-all-start.3 = ((f32[8,2,128,256]{3,2,1,0:T(8,128)}), f32[8,2,128,256]{3,2,1,0:T(8,128)S(1)}, u32[]{:S(2)}, u32[]{:S(2)}) async-start(f32[8,2,128,256]{3,2,1,0:T(8,128)} %fusion.40), calls=%async_computation.3 | async-start | bytes 4194304 | tf_op jit(solution)/shard_map/all_to_all | solution.py:346
  118.4 156.9 %all-reduce.5.cloned.1.call-start = ((), (), s32[]{:S(2)}) async-start(), calls=%async_computation.5 | async-start | bytes 4194304 | tf_op jit(solution)/shard_map/psum | solution.py:352
  148.5 1.2 copy-start.2
  185.2 1.0 copy-start.5
  189.3 86.0 %copy-start.1 = (f32[4,128,1024]{2,1,0:T(8,128)S(1)}, f32[4,128,1024]{2,1,0:T(8,128)}, u32[]{:S(2)}) copy-start(f32[4,128,1024]{2,1,0:T(8,128)} %param.6) | copy-start | bytes 6291460
Sparse Core Ops, SparseCore 0:
  189.5 85.8 all-reduce.4
where the time goes:
time: 286 us
  waiting for transfers between devices  158 us (55%)
  other arithmetic  38.9 us (14%)
  blocking collectives  29 us (10%)
  matrix products  17.6 us (6%)
  starting transfers between devices  16.7 us (6%)
  between operations  14.8 us (5%)
  local copies, waits for them, and re-layouts  9.96 us (3%)
    psum x1, waiting for transfers between devices, shards(): summed = lax.psum(log_terms, 'view')  86 us
    all_to_all x2, waiting for transfers between devices, to_columns_blocked(): lax.all_to_all(spectra, 'slab', split_axis=0, concat_axis=0, tiled=True)  30.1 us
    all_to_all x1, blocking collectives, convolve(): lax.all_to_all(planes, 'slab', split_axis=0, concat_axis=0, tiled=True)  29 us
    all_to_all x1, waiting for transfers between devices, shards(): lax.all_to_all(spectra, 'slab', split_axis=0, concat_axis=0, tiled=True)  24 us
    all_to_all x1, waiting for transfers between devices, convolve(): lax.all_to_all(planes, 'slab', split_axis=0, concat_axis=0, tiled=True)  18.4 us
    unnamed x82, other arithmetic  14.6 us
    all_to_all x2, starting transfers between devices, to_columns_blocked(): lax.all_to_all(spectra, 'slab', split_axis=0, concat_axis=0, tiled=True)  8.95 us
    dot_general x5, matrix products, lane_stage(): jnp.einsum('...j,jn->...n', joined, matrix, precision=lax.Precision.HIGH)  8.46 us
  transfers between devices with their start and end apart: 5, of which 5 were waited for; matrix products, arithmetic and copies ran while one was open for 7% of the time, Pallas kernels for 0%

commit v1 on v0

--- a/solution.py
+++ b/solution.py
@@ -5,6 +5,29 @@
 from jax.sharding import PartitionSpec as P
 
 highest = lax.Precision.HIGHEST
+
+
+def in_blocks(x, dim, count):
+    shape = x.shape
+    blocks = x.reshape(*shape[:dim], count, shape[dim] // count, *shape[dim + 1 :])
+    return jnp.moveaxis(blocks, dim, 0)
+
+
+def laid_out(parts, dim):
+    shape = list(parts.shape[1:])
+    shape[dim] *= parts.shape[0]
+    return jnp.moveaxis(parts, 0, dim).reshape(shape)
+
+
+def pairwise_exchange(value, axis, split_dim, concat_dim):
+    size, mine = (lax.axis_size(axis), lax.axis_index(axis))
+    blocks = in_blocks(value, split_dim, size)
+    done = [blocks[mine]]
+    for hop in range(1, size):
+        sent = blocks[mine ^ hop]
+        done.append(lax.ppermute(sent, axis, [(i, i ^ hop) for i in range(size)]))
+    blocks = jnp.stack(done)[mine ^ jnp.arange(size)]
+    return laid_out(blocks, concat_dim)
 
 
 def block_matrix(multiplier, shifting, weights):
@@ -343,7 +366,7 @@
     blurred = convolve(spectra, transfer_imag)
     quotient = to_blocks(views[0], block_count) / blurred
     spectra = depth_forward(quotient, depth)
-    spectra = lax.all_to_all(spectra, "slab", split_axis=0, concat_axis=0, tiled=True)
+    spectra = pairwise_exchange(spectra, "slab", 0, 0)
     spectra = width_forward(spectra, width)
     smeared = convolve(spectra, -transfer_imag)
     correction = jnp.einsum("apxm,aml->apxl", smeared, doubled, precision=lax.Precision.HIGH)

time: 286 us -> 296 us (1.035)
  waiting for transfers between devices: 158 us -> 147 us
  other arithmetic: 38.9 us -> 49.8 us
  local copies, waits for them, and re-layouts: 9.96 us -> 18.6 us
    all_to_all x1 -> x0, waiting for transfers between devices: 24 us -> none  [shards(): lax.all_to_all(spectra, 'slab', split_axis=0, concat_axis=0, tiled=True)]
    ppermute x0 -> x7, waiting for transfers between devices: none -> 21.4 us  [pairwise_exchange(): done.append(lax.ppermute(sent, axis, [(i, i ^ hop) for i in range(size)]))]
    all_to_all x2, waiting for transfers between devices: 30.1 us -> 22.4 us  [to_columns_blocked(): lax.all_to_all(spectra, 'slab', split_axis=0, concat_axis=0, tiled=True)]
    unnamed x26 -> x81, local copies, waits for them, and re-layouts: 4.88 us -> 9.97 us
    unnamed x82 -> x83, other arithmetic: 14.6 us -> 18.9 us
    ppermute x0 -> x7, starting transfers between devices: none -> 4.15 us  [pairwise_exchange(): done.append(lax.ppermute(sent, axis, [(i, i ^ hop) for i in range(size)]))]
    all_to_all x1 -> x0, starting transfers between devices: 3.6 us -> none  [shards(): lax.all_to_all(spectra, 'slab', split_axis=0, concat_axis=0, tiled=True)]
  transfers between devices with their start and end apart: 5 -> 11, of which waited for: 5 -> 6; matrix products, arithmetic and copies ran while one was open for 7% -> 12% of each run, Pallas kernels for 0% -> 0%
where the time goes in v1:
time: 296 us; the launch traced here: 295 us
  waiting for transfers between devices  147 us (50%)
  other arithmetic  49.8 us (17%)
  blocking collectives  29 us (10%)
  local copies, waits for them, and re-layouts  18.6 us (6%)
  matrix products  17.9 us (6%)
  starting transfers between devices  17.4 us (6%)
  between operations  15.1 us (5%)
    psum x1, waiting for transfers between devices, shards(): summed = lax.psum(log_terms, 'view')  86 us
    all_to_all x1, blocking collectives, convolve(): lax.all_to_all(planes, 'slab', split_axis=0, concat_axis=0, tiled=True)  29 us
    all_to_all x2, waiting for transfers between devices, to_columns_blocked(): lax.all_to_all(spectra, 'slab', split_axis=0, concat_axis=0, tiled=True)  22.4 us
    ppermute x7, waiting for transfers between devices, pairwise_exchange(): done.append(lax.ppermute(sent, axis, [(i, i ^ hop) for i in range(size)]))  21.4 us
    unnamed x83, other arithmetic  18.9 us
    all_to_all x1, waiting for transfers between devices, convolve(): lax.all_to_all(planes, 'slab', split_axis=0, concat_axis=0, tiled=True)  17.2 us
    unnamed x81, local copies, waits for them, and re-layouts  9.97 us
    all_to_all x2, starting transfers between devices, to_columns_blocked(): lax.all_to_all(spectra, 'slab', split_axis=0, concat_axis=0, tiled=True)  9.36 us
  transfers between devices with their start and end apart: 11, of which 6 were waited for; matrix products, arithmetic and copies ran while one was open for 12% of the time, Pallas kernels for 0%

profile of v1, /device:TPU:0, one launch (start us, length us, event | category | flops | bytes accessed | tf_op | source)
XLA Modules:
  0.0 294.8 jit_solution(15101042439127880588)
XLA Ops:
  7.2 1.3 copy.41
  9.6 1.6 convolution_bitcast_fusion
  11.2 5.2 %all-to-all-start.1 = ((f32[8,1,128,256]{3,2,1,0:T(8,128)}), f32[8,1,128,256]{3,2,1,0:T(8,128)S(1)}, u32[]{:S(2)}, u32[]{:S(2)}) async-start(f32[8,1,128,256]{3,2,1,0:T(8,128)} %convolution_bitcast_fusion), calls=%async_computation.1 | async-start | bytes 2097152 | tf_op jit(solution)/shard_map/all_to_all | solution.py:351
  27.1 2.0 constant_dynamic-update-slice_fusion
  29.1 1.7 slice_negate_fusion.13
  30.9 4.0 %fusion.26 = f32[8,2,128,256]{3,2,1,0:T(8,128)} fusion(f32[8,2,128,128]{3,2,1,0:T(8,128)S(1)} %get-tuple-element.152, f32[8,2,128,128]{3,2,1,0:T(8,128)S(1)} %get-tuple-element.151, f32[8,2,128,256]{3,2,1,0:T(8,128)} %constant_dynamic-update-slice_fusion, f32[8,256]{1,0:T(8,128)S(1)} %copy-done.23, f32[8,256]{1,0:T(8,128)S(1)} %get-tuple-element.355, ...), kind=kOutput, calls=%fused_computation.39 | convolution fusion | flops 807600128 | bytes 6504448 | tf_op jit(solution)/shard_map/...j,jn->...n/dot_general | solution.py:258
  34.9 4.2 %all-to-all-start = ((f32[8,2,128,256]{3,2,1,0:T(8,128)}), f32[8,2,128,256]{3,2,1,0:T(8,128)S(1)}, u32[]{:S(2)}, u32[]{:S(2)}) async-start(f32[8,2,128,256]{3,2,1,0:T(8,128)} %fusion.26), calls=%async_computation | async-start | bytes 4194304 | tf_op jit(solution)/shard_map/all_to_all | solution.py:351
  42.3 1.0 maximum_bitcast_fusion.7
  43.3 22.4 %all-to-all-done = f32[8,2,128,256]{3,2,1,0:T(8,128)S(1)} async-done(((f32[8,2,128,256]{3,2,1,0:T(8,128)}), f32[8,2,128,256]{3,2,1,0:T(8,128)S(1)}, u32[]{:S(2)}, u32[]{:S(2)}) %all-to-all-start) | async-done | bytes 2097184 | tf_op jit(solution)/shard_map/all_to_all | solution.py:351
  67.7 1.6 fusion.66
  71.7 1.5 fusion.63
  81.0 3.6 %all-to-all-start.2 = ((f32[8,2,128,256]{3,2,1,0:T(8,128)}), f32[8,2,128,256]{3,2,1,0:T(8,128)S(1)}, u32[]{:S(2)}, u32[]{:S(2)}) async-start(f32[8,2,128,256]{3,2,1,0:T(8,128)} %constant_dynamic-update-slice_fusion.40), calls=%async_computation.2 | async-start | bytes 4194304 | tf_op jit(solution)/shard_map/all_to_all | solution.py:363
  86.2 1.7 fusion.270
  93.9 17.2 %all-to-all-done.2 = f32[8,2,128,256]{3,2,1,0:T(8,128)S(1)} async-done(((f32[8,2,128,256]{3,2,1,0:T(8,128)}), f32[8,2,128,256]{3,2,1,0:T(8,128)S(1)}, u32[]{:S(2)}, u32[]{:S(2)}) %all-to-all-start.2) | async-done | bytes 2097184 | tf_op jit(solution)/shard_map/all_to_all | solution.py:363
  114.3 2.0 div.9
  118.3 1.1 fusion.40
  119.4 1.3 constant_dynamic-slice_fusion
  120.7 2.4 maximum_negate_fusion
  123.7 1.4 collective-permute-start.2
  125.6 1.1 collective-permute-start.4
  128.2 4.1 %collective-permute-done.1 = f32[1,2,128,256]{3,2,1,0:T(8,128)S(1)} collective-permute-done((f32[1,2,128,256]{3,2,1,0:T(8,128)}, f32[1,2,128,256]{3,2,1,0:T(8,128)S(1)}, u32[]{:S(2)}, u32[]{:S(2)}) %collective-permute-start.1) | collective-permute-done | bytes 262176 | tf_op jit(solution)/shard_map/ppermute | solution.py:28
  132.4 4.8 %collective-permute-done.2 = f32[1,2,128,256]{3,2,1,0:T(8,128)S(1)} collective-permute-done((f32[1,2,128,256]{3,2,1,0:T(8,128)S(1)}, f32[1,2,128,256]{3,2,1,0:T(8,128)S(1)}, u32[]{:S(2)}, u32[]{:S(2)}) %collective-permute-start.2) | collective-permute-done | bytes 262176 | tf_op jit(solution)/shard_map/ppermute | solution.py:28
  137.3 12.4 %collective-permute-done.4 = f32[1,2,128,256]{3,2,1,0:T(8,128)S(1)} collective-permute-done((f32[1,2,128,256]{3,2,1,0:T(8,128)S(1)}, f32[1,2,128,256]{3,2,1,0:T(8,128)S(1)}, u32[]{:S(2)}, u32[]{:S(2)}) %collective-permute-start.4) | collective-permute-done | bytes 262176 | tf_op jit(solution)/shard_map/ppermute | solution.py:28
  149.9 1.3 copy-done.8
  151.2 2.3 gather_fusion
  155.4 1.6 fusion.60
  158.8 1.5 fusion.57
  162.6 29.0 %all_to_all.20 = f32[8,2,128,256]{3,2,1,0:T(8,128)S(1)} all-to-all(f32[8,2,128,256]{3,2,1,0:T(8,128)S(1)} %constant_dynamic-update-slice_fusion.80), channel_id=1, replica_groups=mesh['slab'=8,'view'=4] {'slab'}, dimensions={0} | all-to-all | bytes 4194304 | tf_op jit(solution)/shard_map/all_to_all | solution.py:363
  195.5 1.1 fusion.54
  197.1 1.5 copy.69
  198.6 86.0 %all-reduce.5.cloned.1.call-done = f32[4,128,1024]{2,1,0:T(8,128)} async-done(((f32[4,128,1024]{2,1,0:T(8,128)}), f32[4,128,1024]{2,1,0:T(8,128)}) %all-reduce.5.cloned.1.call-update) | async-done | bytes 2097168 | tf_op jit(solution)/shard_map/psum | solution.py:375
  284.7 3.3 %exponential_multiply_fusion = f32[4,128,1024]{2,1,0:T(8,128)} fusion(f32[4,128,1024]{2,1,0:T(8,128)S(1)} %copy-done.1, f32[4,128,1024]{2,1,0:T(8,128)} %all-reduce.5.cloned.1.call-done), kind=kLoop, calls=%fused_computation.70 | loop fusion | flops 1048576 | bytes 6291456 | tf_op jit(solution)/shard_map/mul | solution.py:376
  (317 shorter events, 52.6 us)
Async XLA Ops:
  7.2 2.4 copy-start.12
  9.5 1.7 copy-start.22
  9.5 7.7 %copy-start = (f32[4,128,1024]{2,1,0:T(8,128)S(1)}, f32[4,128,1024]{2,1,0:T(8,128)}, u32[]{:S(2)}) copy-start(f32[4,128,1024]{2,1,0:T(8,128)} %param.6) | copy-start | bytes 6291460
  11.2 23.7 %all-to-all-start.1 = ((f32[8,1,128,256]{3,2,1,0:T(8,128)}), f32[8,1,128,256]{3,2,1,0:T(8,128)S(1)}, u32[]{:S(2)}, u32[]{:S(2)}) async-start(f32[8,1,128,256]{3,2,1,0:T(8,128)} %convolution_bitcast_fusion), calls=%async_computation.1 | async-start | bytes 2097152 | tf_op jit(solution)/shard_map/all_to_all | solution.py:351
  21.5 3.5 %copy-start.4 = (f32[1,2,128,128]{3,2,1,0:T(8,128)}, f32[1,2,128,128]{3,2,1,0:T(8,128)S(1)}, u32[]{:S(2)}) copy-start(f32[1,2,128,128]{3,2,1,0:T(8,128)S(1)} %get-tuple-element.303) | copy-start | bytes 393220
  21.5 3.4 %copy-start.5 = (f32[1,2,128,128]{3,2,1,0:T(8,128)}, f32[1,2,128,128]{3,2,1,0:T(8,128)S(1)}, u32[]{:S(2)}) copy-start(f32[1,2,128,128]{3,2,1,0:T(8,128)S(1)} %get-tuple-element.304) | copy-start | bytes 393220
  21.7 3.3 %copy-start.6 = (f32[1,2,128,128]{3,2,1,0:T(8,128)}, f32[1,2,128,128]{3,2,1,0:T(8,128)S(1)}, u32[]{:S(2)}) copy-start(f32[1,2,128,128]{3,2,1,0:T(8,128)S(1)} %get-tuple-element.309) | copy-start | bytes 393220
  21.7 3.3 %copy-start.7 = (f32[1,2,128,128]{3,2,1,0:T(8,128)}, f32[1,2,128,128]{3,2,1,0:T(8,128)S(1)}, u32[]{:S(2)}) copy-start(f32[1,2,128,128]{3,2,1,0:T(8,128)S(1)} %get-tuple-element.310) | copy-start | bytes 393220
  21.7 2.4 copy-start.10
  21.8 2.4 copy-start.11
  29.1 1.7 copy-start.13
  29.1 1.7 copy-start.23
  34.9 30.8 %all-to-all-start = ((f32[8,2,128,256]{3,2,1,0:T(8,128)}), f32[8,2,128,256]{3,2,1,0:T(8,128)S(1)}, u32[]{:S(2)}, u32[]{:S(2)}) async-start(f32[8,2,128,256]{3,2,1,0:T(8,128)} %fusion.26), calls=%async_computation | async-start | bytes 4194304 | tf_op jit(solution)/shard_map/all_to_all | solution.py:351
  69.3 1.2 copy-start.3
  81.0 30.2 %all-to-all-start.2 = ((f32[8,2,128,256]{3,2,1,0:T(8,128)}), f32[8,2,128,256]{3,2,1,0:T(8,128)S(1)}, u32[]{:S(2)}, u32[]{:S(2)}) async-start(f32[8,2,128,256]{3,2,1,0:T(8,128)} %constant_dynamic-update-slice_fusion.40), calls=%async_computation.2 | async-start | bytes 4194304 | tf_op jit(solution)/shard_map/all_to_all | solution.py:363
  84.6 200.1 %all-reduce.5.cloned.1.call-start = ((), (), s32[]{:S(2)}) async-start(), calls=%async_computation.4 | async-start | bytes 4194304 | tf_op jit(solution)/shard_map/psum | solution.py:375
  119.4 1.3 copy-start.31
  120.7 6.0 %collective-permute-start = (f32[1,2,128,256]{3,2,1,0:T(8,128)}, f32[1,2,128,256]{3,2,1,0:T(8,128)}, u32[]{:S(2)}, u32[]{:S(2)}) collective-permute-start(f32[1,2,128,256]{3,2,1,0:T(8,128)} %get-tuple-element.112), channel_id=1, source_target_pairs={{0,4},{4,0},{8,12},{12,8},{16,20},{20,16},{24,28},{28,24},{1,5},{5... | collective-permute-start | bytes 786440 | tf_op jit(solution)/shard_map/ppermute | solution.py:28
  120.7 3.0 %copy-start.21 = (f32[1,2,128,256]{3,2,1,0:T(8,128)S(1)}, f32[1,2,128,256]{3,2,1,0:T(8,128)}, u32[]{:S(2)}) copy-start(f32[1,2,128,256]{3,2,1,0:T(8,128)} %get-tuple-element.110) | copy-start | bytes 786436
  120.7 4.4 %copy-start.20 = (f32[1,2,128,256]{3,2,1,0:T(8,128)S(1)}, f32[1,2,128,256]{3,2,1,0:T(8,128)}, u32[]{:S(2)}) copy-start(f32[1,2,128,256]{3,2,1,0:T(8,128)} %get-tuple-element.109) | copy-start | bytes 786436
  120.7 4.9 %copy-start.19 = (f32[1,2,128,256]{3,2,1,0:T(8,128)S(1)}, f32[1,2,128,256]{3,2,1,0:T(8,128)}, u32[]{:S(2)}) copy-start(f32[1,2,128,256]{3,2,1,0:T(8,128)} %get-tuple-element.108) | copy-start | bytes 786436
  120.7 6.0 %copy-start.18 = (f32[1,2,128,256]{3,2,1,0:T(8,128)S(1)}, f32[1,2,128,256]{3,2,1,0:T(8,128)}, u32[]{:S(2)}) copy-start(f32[1,2,128,256]{3,2,1,0:T(8,128)} %get-tuple-element.107) | copy-start | bytes 786436
  120.7 11.7 %copy-start.17 = (f32[1,2,128,256]{3,2,1,0:T(8,128)S(1)}, f32[1,2,128,256]{3,2,1,0:T(8,128)}, u32[]{:S(2)}) copy-start(f32[1,2,128,256]{3,2,1,0:T(8,128)} %get-tuple-element.106) | copy-start | bytes 786436
  123.1 9.3 %collective-permute-start.1 = (f32[1,2,128,256]{3,2,1,0:T(8,128)}, f32[1,2,128,256]{3,2,1,0:T(8,128)S(1)}, u32[]{:S(2)}, u32[]{:S(2)}) collective-permute-start(f32[1,2,128,256]{3,2,1,0:T(8,128)} %get-tuple-element.111), channel_id=1, source_target_pairs={{0,8},{4,12},{8,0},{12,4},{16,24},{20,28},{24,16},{28,20},{1,9},{5... | collective-permute-start | bytes 786440 | tf_op jit(solution)/shard_map/ppermute | solution.py:28
  123.7 13.6 %collective-permute-start.2 = (f32[1,2,128,256]{3,2,1,0:T(8,128)S(1)}, f32[1,2,128,256]{3,2,1,0:T(8,128)S(1)}, u32[]{:S(2)}, u32[]{:S(2)}) collective-permute-start(f32[1,2,128,256]{3,2,1,0:T(8,128)S(1)} %copy-done.21), channel_id=1, source_target_pairs={{0,12},{4,8},{8,4},{12,0},{16,28},{20,24},{24,20},{28,16},{1,13},{... | collective-permute-start | bytes 786440 | tf_op jit(solution)/shard_map/ppermute | solution.py:28
  125.0 12.2 %collective-permute-start.3 = (f32[1,2,128,256]{3,2,1,0:T(8,128)S(1)}, f32[1,2,128,256]{3,2,1,0:T(8,128)S(1)}, u32[]{:S(2)}, u32[]{:S(2)}) collective-permute-start(f32[1,2,128,256]{3,2,1,0:T(8,128)S(1)} %copy-done.20), channel_id=1, source_target_pairs={{0,16},{4,20},{8,24},{12,28},{16,0},{20,4},{24,8},{28,12},{1,17},{... | collective-permute-start | bytes 786440 | tf_op jit(solution)/shard_map/ppermute | solution.py:28
  125.6 24.2 %collective-permute-start.4 = (f32[1,2,128,256]{3,2,1,0:T(8,128)S(1)}, f32[1,2,128,256]{3,2,1,0:T(8,128)S(1)}, u32[]{:S(2)}, u32[]{:S(2)}) collective-permute-start(f32[1,2,128,256]{3,2,1,0:T(8,128)S(1)} %copy-done.19), channel_id=1, source_target_pairs={{0,20},{4,16},{8,28},{12,24},{16,4},{20,0},{24,12},{28,8},{1,21},{... | collective-permute-start | bytes 786440 | tf_op jit(solution)/shard_map/ppermute | solution.py:28
  126.7 23.1 %collective-permute-start.5 = (f32[1,2,128,256]{3,2,1,0:T(8,128)S(1)}, f32[1,2,128,256]{3,2,1,0:T(8,128)S(1)}, u32[]{:S(2)}, u32[]{:S(2)}) collective-permute-start(f32[1,2,128,256]{3,2,1,0:T(8,128)S(1)} %copy-done.18), channel_id=1, source_target_pairs={{0,24},{4,28},{8,16},{12,20},{16,8},{20,12},{24,0},{28,4},{1,25},{... | collective-permute-start | bytes 786440 | tf_op jit(solution)/shard_map/ppermute | solution.py:28
  132.4 17.4 %collective-permute-start.6 = (f32[1,2,128,256]{3,2,1,0:T(8,128)S(1)}, f32[1,2,128,256]{3,2,1,0:T(8,128)S(1)}, u32[]{:S(2)}, u32[]{:S(2)}) collective-permute-start(f32[1,2,128,256]{3,2,1,0:T(8,128)S(1)} %copy-done.17), channel_id=1, source_target_pairs={{0,28},{4,24},{8,20},{12,16},{16,12},{20,8},{24,4},{28,0},{1,29},{... | collective-permute-start | bytes 786440 | tf_op jit(solution)/shard_map/ppermute | solution.py:28
  149.8 1.3 copy-start.8
  156.9 1.2 copy-start.2
  198.6 86.1 %copy-start.1 = (f32[4,128,1024]{2,1,0:T(8,128)S(1)}, f32[4,128,1024]{2,1,0:T(8,128)}, u32[]{:S(2)}) copy-start(f32[4,128,1024]{2,1,0:T(8,128)} %param.6) | copy-start | bytes 6291460
  (12 other events, 9.4 us)
Sparse Core Ops, SparseCore 0:
  198.7 85.8 all-reduce.4
